TPU v7x, 512 devices: a whole 4x4x16 slice. The times are simulated.
512 devices in a mesh: chan: 32 (over y, z_lo), inp: 16 (over z_hi, x, core).
Axes of the slice: x: 4, y: 4, z: 16 (z_hi: 2, z_lo: 8; z = z_hi * 8 + z_lo), core: 2. Of those that a mesh axis runs over, the one named last changes fastest.
Arguments:
- voltages: int32 [512, 524288], P('inp', 'chan'), may hold values from -128 to 127
- scales: int32 [512], P('inp'), may hold values from 1 to 5
Outputs:
- visibilities: bfloat16 [2, 1024, 512, 512], P(None, 'chan', 'inp')
All inputs are finite; a program needn't handle non-finite values.
Results may differ from a plain program's by a relative error of at most 0.0069.
Values may be sent and summed in bfloat16 or wider, within the bound.
No kernel may reach another device: no remote copies, remote signals or barrier semaphores. Data moves between devices by JAX's collectives and lax.ppermute only.
A program may use at most 128 MiB of HBM per device.

v0:
```python
import math
import jax
import jax.numpy as jnp
from jax import lax
from jax.sharding import PartitionSpec as P

NFFT = 4096
CHANS = 1024
TAPS = 8


def shifted(block, axis, distance):
    devices = range(lax.axis_size(axis))
    route = [(i - distance, i) for i in devices if i - distance in devices]
    return lax.ppermute(block, axis, route)


def window_table():
    count = TAPS * NFFT
    places = jnp.arange(count).astype(jnp.float32)
    shaping = jnp.sinc((places - count / 2.0) / NFFT)
    taper = 0.5 - 0.5 * jnp.cos(2.0 * math.pi * places / count)
    return (shaping * taper).reshape(TAPS, NFFT)


def dft_table():
    columns = jnp.arange(CHANS, dtype=jnp.int32)
    norm_factor = 1.0 / math.sqrt(NFFT)

    def one_block(start):
        rows_idx = start + jnp.arange(512, dtype=jnp.int32)
        phase = rows_idx[:, None] * columns[None, :] % NFFT
        angle = phase.astype(jnp.float32) * (2.0 * math.pi / NFFT)
        return jnp.stack(
            [jnp.cos(angle) * norm_factor, -jnp.sin(angle) * norm_factor], axis=1
        ).astype(jnp.bfloat16)

    starts = jnp.arange(NFFT // 512, dtype=jnp.int32) * 512
    return lax.map(one_block, starts).reshape(NFFT, 2, CHANS)


def filter_taps(padded, window, spec_count):
    total = jnp.zeros((padded.shape[0], spec_count, NFFT), jnp.float32)
    for tap_index in range(TAPS):
        total = total + window[tap_index] * padded[:, tap_index : tap_index + spec_count]
    return total.astype(jnp.bfloat16)


def shards(voltages, scales):
    inp_count = voltages.shape[0]
    shard_len = voltages.shape[1]
    spec_count = shard_len // NFFT
    history_len = (TAPS - 1) * NFFT
    reach_back = -(-history_len // shard_len)
    samples = voltages.astype(jnp.bfloat16)
    earlier = []
    for distance in range(1, reach_back + 1):
        take_count = min(shard_len, history_len - (distance - 1) * shard_len)
        received = shifted(samples[:, shard_len - take_count :], "chan", distance)
        earlier = [received] + earlier
    joined = jnp.concatenate(earlier + [samples], axis=1).astype(jnp.float32)
    signal = joined * scales.astype(jnp.float32)[:, None] * (1.0 / 256.0)
    padded = signal.reshape(inp_count, TAPS - 1 + spec_count, NFFT)
    filtered = filter_taps(padded, window_table(), spec_count)
    spectra = jnp.einsum(
        "isn,nrc->cirs", filtered, dft_table(), preferred_element_type=jnp.float32
    ).astype(jnp.bfloat16)
    local_block = lax.all_to_all(spectra, "chan", split_axis=0, concat_axis=3, tiled=True)
    chan_count = local_block.shape[0]
    spec_total = local_block.shape[3]
    own_rows = local_block.reshape(chan_count, inp_count, 2 * spec_total)
    swapped = jnp.concatenate([own_rows[..., spec_total:], -own_rows[..., :spec_total]], axis=-1)
    piece = lax.all_gather(own_rows, "inp", axis=1, tiled=True)
    real_part = jnp.einsum("cik,cjk->cij", own_rows, piece, preferred_element_type=jnp.float32)
    imag_part = jnp.einsum("cik,cjk->cij", swapped, piece, preferred_element_type=jnp.float32)
    result = jnp.stack([real_part, imag_part]) * (1.0 / spec_total)
    return result.astype(jnp.bfloat16)


def solution(mesh):
    placed = (P("inp", "chan"), P("inp"))
    return jax.shard_map(
        shards, mesh=mesh, in_specs=placed, out_specs=P(None, "chan", "inp", None), check_vma=False
    )
```

profile of v0, /device:TPU:1, one launch (start us, length us, event | category | flops | bytes accessed | tf_op | source)
XLA Modules:
  0.0 408.2 jit_solution(11215632262744515466)
XLA Ops:
  6.5 0.0 all-gather.2.cloned.1.call-start
  6.5 1.7 convert_element_type.91
  8.2 4.4 %collective-permute-start.1 = (bf16[32,16384]{1,0:T(8,128)(2,1)S(1)}, bf16[32,16384]{1,0:T(8,128)(2,1)S(1)}, u32[]{:S(2)}, u32[]{:S(2)}) collective-permute-start(bf16[32,16384]{1,0:T(8,128)(2,1)S(1)} %convert_element_type.91), channel_id=1, source_target_pairs={{0,16},{16,32},{32,48},{48,64},{64,80},{80,96},{96,112},{112,128},... | collective-permute-start | bytes 3145736 | tf_op jit(solution)/shard_map/ppermute | solution.py:15
  12.7 0.9 slice.85
  13.6 4.9 %collective-permute-start = (bf16[32,12288]{1,0:T(8,128)(2,1)}, bf16[32,12288]{1,0:T(8,128)(2,1)S(1)}, u32[]{:S(2)}, u32[]{:S(2)}) collective-permute-start(bf16[32,12288]{1,0:T(8,128)(2,1)} %slice.85), channel_id=1, source_target_pairs={{0,32},{16,48},{32,64},{48,80},{64,96},{80,112},{96,128},{112,144}... | collective-permute-start | bytes 2359304 | tf_op jit(solution)/shard_map/ppermute | solution.py:15
  18.5 0.0 copy-start.1
  18.5 95.0 %while.13 = (s32[]{:T(128)}, bf16[8,512,2,1024]{3,1,0,2:T(8,128)(2,1)}, s32[8]{0:T(128)S(1)}, s32[]{:T(128)}) while((s32[]{:T(128)}, bf16[8,512,2,1024]{3,1,0,2:T(8,128)(2,1)}, s32[8]{0:T(128)S(1)}, s32[]{:T(128)}) %tuple.40), condition=%wide.region_1.2_spmd.clone, body=%wide.region_0.1_spmd.clone.sunk | while | flops 14156290 | bytes 6295633 | solution.py:39
  18.5 0.6 dynamic_slice.9
  19.2 0.6 iota_add_fusion.2
  19.8 9.1 %fusion.48 = (bf16[1,512,1,1024]{3,1,2,0:T(8,128)(2,1)S(1)}, bf16[1,512,1,1024]{3,1,2,0:T(8,128)(2,1)S(1)}) fusion(s32[512]{0:T(512)S(1)} %iota_add_fusion.2), kind=kLoop, calls=%fused_computation.15.clone.1 | loop fusion | flops 9961472 | bytes 2099200 | tf_op jit(solution)/shard_map/while/body/eval_jaxpr/stack | solution.py:34
  28.9 1.6 fusion.49
  30.5 0.6 dynamic_slice.9
  31.1 0.6 iota_add_fusion.2
  31.7 9.1 %fusion.48 = (bf16[1,512,1,1024]{3,1,2,0:T(8,128)(2,1)S(1)}, bf16[1,512,1,1024]{3,1,2,0:T(8,128)(2,1)S(1)}) fusion(s32[512]{0:T(512)S(1)} %iota_add_fusion.2), kind=kLoop, calls=%fused_computation.15.clone.1 | loop fusion | flops 9961472 | bytes 2099200 | tf_op jit(solution)/shard_map/while/body/eval_jaxpr/stack | solution.py:34
  40.8 1.5 fusion.49
  42.3 0.6 dynamic_slice.9
  42.9 0.6 iota_add_fusion.2
  43.6 9.1 %fusion.48 = (bf16[1,512,1,1024]{3,1,2,0:T(8,128)(2,1)S(1)}, bf16[1,512,1,1024]{3,1,2,0:T(8,128)(2,1)S(1)}) fusion(s32[512]{0:T(512)S(1)} %iota_add_fusion.2), kind=kLoop, calls=%fused_computation.15.clone.1 | loop fusion | flops 9961472 | bytes 2099200 | tf_op jit(solution)/shard_map/while/body/eval_jaxpr/stack | solution.py:34
  52.7 1.5 fusion.49
  54.2 0.6 dynamic_slice.9
  54.8 0.6 iota_add_fusion.2
  55.5 9.1 %fusion.48 = (bf16[1,512,1,1024]{3,1,2,0:T(8,128)(2,1)S(1)}, bf16[1,512,1,1024]{3,1,2,0:T(8,128)(2,1)S(1)}) fusion(s32[512]{0:T(512)S(1)} %iota_add_fusion.2), kind=kLoop, calls=%fused_computation.15.clone.1 | loop fusion | flops 9961472 | bytes 2099200 | tf_op jit(solution)/shard_map/while/body/eval_jaxpr/stack | solution.py:34
  64.6 1.5 fusion.49
  66.0 0.6 dynamic_slice.9
  66.7 0.6 iota_add_fusion.2
  67.3 9.1 %fusion.48 = (bf16[1,512,1,1024]{3,1,2,0:T(8,128)(2,1)S(1)}, bf16[1,512,1,1024]{3,1,2,0:T(8,128)(2,1)S(1)}) fusion(s32[512]{0:T(512)S(1)} %iota_add_fusion.2), kind=kLoop, calls=%fused_computation.15.clone.1 | loop fusion | flops 9961472 | bytes 2099200 | tf_op jit(solution)/shard_map/while/body/eval_jaxpr/stack | solution.py:34
  76.4 1.5 fusion.49
  78.0 0.6 dynamic_slice.9
  78.6 0.6 iota_add_fusion.2
  79.2 9.1 %fusion.48 = (bf16[1,512,1,1024]{3,1,2,0:T(8,128)(2,1)S(1)}, bf16[1,512,1,1024]{3,1,2,0:T(8,128)(2,1)S(1)}) fusion(s32[512]{0:T(512)S(1)} %iota_add_fusion.2), kind=kLoop, calls=%fused_computation.15.clone.1 | loop fusion | flops 9961472 | bytes 2099200 | tf_op jit(solution)/shard_map/while/body/eval_jaxpr/stack | solution.py:34
  88.3 1.5 fusion.49
  89.8 0.6 dynamic_slice.9
  90.4 0.6 iota_add_fusion.2
  91.1 9.1 %fusion.48 = (bf16[1,512,1,1024]{3,1,2,0:T(8,128)(2,1)S(1)}, bf16[1,512,1,1024]{3,1,2,0:T(8,128)(2,1)S(1)}) fusion(s32[512]{0:T(512)S(1)} %iota_add_fusion.2), kind=kLoop, calls=%fused_computation.15.clone.1 | loop fusion | flops 9961472 | bytes 2099200 | tf_op jit(solution)/shard_map/while/body/eval_jaxpr/stack | solution.py:34
  100.2 1.5 fusion.49
  101.6 0.6 dynamic_slice.9
  102.3 0.6 iota_add_fusion.2
  102.9 9.1 %fusion.48 = (bf16[1,512,1,1024]{3,1,2,0:T(8,128)(2,1)S(1)}, bf16[1,512,1,1024]{3,1,2,0:T(8,128)(2,1)S(1)}) fusion(s32[512]{0:T(512)S(1)} %iota_add_fusion.2), kind=kLoop, calls=%fused_computation.15.clone.1 | loop fusion | flops 9961472 | bytes 2099200 | tf_op jit(solution)/shard_map/while/body/eval_jaxpr/stack | solution.py:34
  112.0 1.5 fusion.49
  113.5 0.0 copy-done.1
  113.5 0.6 fusion.30
  114.1 0.0 collective-permute-done
  114.1 0.0 collective-permute-done.1
  114.1 2.9 maximum_convert_fusion
  117.1 6.8 %reshape.221 = f32[32,11,4096]{2,1,0:T(8,128)} reshape(f32[32,45056]{1,0:T(8,128)} %maximum_convert_fusion) | data formatting | bytes 11534336 | tf_op jit(solution)/shard_map/convert_element_type | solution.py:61
  123.9 8.3 %multiply_multiply_fusion = f32[32,11,4096]{2,1,0:T(8,128)} fusion(f32[32,11,4096]{2,1,0:T(8,128)} %reshape.221, f32[32]{0:T(128)S(1)} %convert_element_type.94), kind=kLoop, calls=%fused_computation.18 | loop fusion | flops 2883584 | bytes 11534464 | tf_op jit(solution)/shard_map/mul | solution.py:62
  132.2 18.0 %fusion.13 = bf16[32,4,4096]{2,1,0:T(4,128)(2,1)S(1)} fusion(f32[32,11,4096]{2,1,0:T(8,128)} %multiply_multiply_fusion, f32[4096]{0:T(1024)S(1)} %get-tuple-element.79, f32[4096]{0:T(1024)S(1)} %get-tuple-element.80, f32[4096]{0:T(1024)S(1)} %get-tuple-element.81, f32[4096]{0:T(1024)S(1)} %get-tuple-element.82, f32[4096]{0:T(1024)S(1)} %get-tuple-element.83, ...), kind=kLoop, calls=%fused_computation.24 | loop fusion | flops 8388608 | bytes 17956864 | tf_op jit(solution)/shard_map/convert_element_type | solution.py:46
  150.2 8.7 %fusion.20 = bf16[1024,32,2,4]{0,1,3,2:T(8,128)(2,1)S(1)} fusion(bf16[4096,2,1024,1]{2,0,3,1:T(8,128)(2,1)} %bitcast.42, bf16[32,4,4096]{2,1,0:T(4,128)(2,1)S(1)} %fusion.13), kind=kOutput, calls=%fused_computation.41 | convolution fusion | flops 2147745792 | bytes 18350080 | tf_op jit(solution)/shard_map/isn,nrc->cirs/dot_general | solution.py:65
  158.9 1.4 copy.22
  160.3 2.0 reshape.224
  162.3 40.3 %all_to_all.15 = bf16[32,2,4096]{2,1,0:T(2,128)(2,1)S(1)} all-to-all(bf16[32,2,4096]{2,1,0:T(2,128)(2,1)S(1)} %reshape.224), channel_id=1, replica_groups=mesh['chan'=32,'inp'=16] {'chan'}, dimensions={0} | all-to-all | bytes 1048576 | tf_op jit(solution)/shard_map/all_to_all | solution.py:68
  202.5 1.0 reshape.225
  203.6 1.9 copy.23
  205.5 3.4 copy.25
  208.9 0.0 all-gather.2.cloned.1.call-update
  208.9 1.1 fusion.40
  210.0 180.6 %all-gather.2.cloned.1.call-done = bf16[32,512,256]{2,1,0:T(8,128)(2,1)} async-done(((bf16[32,32,256]{2,1,0:T(8,128)(2,1)}), bf16[32,512,256]{2,1,0:T(8,128)(2,1)}) %all-gather.2.cloned.1.call-update) | async-done | bytes 8388624 | tf_op jit(solution)/shard_map/all_gather | solution.py:73
  390.6 0.0 copy-start
  390.6 6.2 %convolution_bitcast_fusion.1 = f32[1,32,32,512]{3,2,1,0:T(8,128)S(1)} fusion(bf16[32,32,256]{2,1,0:T(8,128)(2,1)} %copy.25, bf16[32,512,256]{2,1,0:T(8,128)(2,1)} %all-gather.2.cloned.1.call-done), kind=kOutput, calls=%fused_computation.39 | convolution fusion | flops 268435456 | bytes 11010048 | tf_op jit(solution)/shard_map/cik,cjk->cij/dot_general | solution.py:74
  396.8 0.0 copy-done
  396.9 2.5 convolution_bitcast_fusion
  399.4 2.0 fusion.11
  (4 shorter events, 0.0 us)
Async XLA Ops:
  6.5 384.1 %all-gather.2.cloned.1.call-start = ((), (), s32[]{:S(2)}) async-start(), calls=%async_computation.1 | async-start | bytes 8912896 | tf_op jit(solution)/shard_map/all_gather | solution.py:73
  8.2 105.9 %collective-permute-start.1 = (bf16[32,16384]{1,0:T(8,128)(2,1)S(1)}, bf16[32,16384]{1,0:T(8,128)(2,1)S(1)}, u32[]{:S(2)}, u32[]{:S(2)}) collective-permute-start(bf16[32,16384]{1,0:T(8,128)(2,1)S(1)} %convert_element_type.91), channel_id=1, source_target_pairs={{0,16},{16,32},{32,48},{48,64},{64,80},{80,96},{96,112},{112,128},... | collective-permute-start | bytes 3145736 | tf_op jit(solution)/shard_map/ppermute | solution.py:15
  13.6 100.5 %collective-permute-start = (bf16[32,12288]{1,0:T(8,128)(2,1)}, bf16[32,12288]{1,0:T(8,128)(2,1)S(1)}, u32[]{:S(2)}, u32[]{:S(2)}) collective-permute-start(bf16[32,12288]{1,0:T(8,128)(2,1)} %slice.85), channel_id=1, source_target_pairs={{0,32},{16,48},{32,64},{48,80},{64,96},{80,112},{96,128},{112,144}... | collective-permute-start | bytes 2359304 | tf_op jit(solution)/shard_map/ppermute | solution.py:15
  18.5 95.0 %copy-start.1 = (s32[32]{0:T(128)S(1)}, s32[32]{0:T(128)}, u32[]{:S(2)}) copy-start(s32[32]{0:T(128)} %param.5) | copy-start | bytes 388
  390.6 6.2 %copy-start = (bf16[32,512,256]{2,1,0:T(8,128)(2,1)S(1)}, bf16[32,512,256]{2,1,0:T(8,128)(2,1)}, u32[]{:S(2)}) copy-start(bf16[32,512,256]{2,1,0:T(8,128)(2,1)} %all-gather.2.cloned.1.call-done) | copy-start | bytes 25165828
Sparse Core Ops, SparseCore 0:
  209.1 181.5 all-gather.1
where the time goes:
time: 409 us; the launch traced here: 408 us
  waiting for transfers between devices  181 us (44%)
  other arithmetic  124 us (30%)
  blocking collectives  40.3 us (10%)
  local copies, waits for them, and re-layouts  22.7 us (6%)
  matrix products  17.4 us (4%)
  between operations  13.5 us (3%)
  starting transfers between devices  9.31 us (2%)
    all_gather x1, waiting for transfers between devices, shards(): piece = lax.all_gather(own_rows, 'inp', axis=1, tiled=True)  181 us
    another operation x8, other arithmetic, one_block(): jnp.stack([jnp.cos(angle) * norm_factor, -jnp.sin(angle) * norm_factor],...  72.7 us
    all_to_all x1, blocking collectives, shards(): lax.all_to_all(spectra, 'chan', split_axis=0, concat_axis=3, tiled=True)  40.3 us
    convert_element_type x1, other arithmetic, filter_taps(): return total.astype(jnp.bfloat16)  18 us
    dynamic_update_slice x8, other arithmetic, dft_table(): return lax.map(one_block, starts).reshape(NFFT, 2, CHANS)  12 us
    ppermute x2, starting transfers between devices, shifted(): return lax.ppermute(block, axis, route)  9.31 us
    dot_general x1, matrix products, shards(): jnp.einsum('isn,nrc->cirs', filtered, dft_table(), preferred_element_type...  8.68 us
    mul x1, other arithmetic, shards(): signal = joined * scales.astype(jnp.float32)[:, None] * (1.0 / 256.0)  8.31 us
  transfers between devices with their start and end apart: 3, of which 1 were waited for; matrix products, arithmetic and copies ran while one was open for 24% of the time, Pallas kernels for 0%

commit v1 on v0

--- a/solution.py
+++ b/solution.py
@@ -7,6 +7,13 @@
 NFFT = 4096
 CHANS = 1024
 TAPS = 8
+
+
+def exchange_gather(shard, axis, d):
+    count = lax.axis_size(axis)
+    blocks = jnp.stack([shard for _ in range(count)])
+    blocks = lax.all_to_all(blocks, axis, split_axis=0, concat_axis=0)
+    return jnp.concatenate(blocks, axis=d)
 
 
 def shifted(block, axis, distance):
@@ -70,7 +77,7 @@
     spec_total = local_block.shape[3]
     own_rows = local_block.reshape(chan_count, inp_count, 2 * spec_total)
     swapped = jnp.concatenate([own_rows[..., spec_total:], -own_rows[..., :spec_total]], axis=-1)
-    piece = lax.all_gather(own_rows, "inp", axis=1, tiled=True)
+    piece = exchange_gather(own_rows, "inp", 1)
     real_part = jnp.einsum("cik,cjk->cij", own_rows, piece, preferred_element_type=jnp.float32)
     imag_part = jnp.einsum("cik,cjk->cij", swapped, piece, preferred_element_type=jnp.float32)
     result = jnp.stack([real_part, imag_part]) * (1.0 / spec_total)

time: 409 us -> 660 us (1.61)
  the two profiles are of different devices: /device:TPU:1 before, /device:TPU:103 now
where the time goes in v1:
time: 660 us; the launch traced here: 659 us
  waiting for transfers between devices  424 us (64%)
  other arithmetic  123 us (19%)
  local copies, waits for them, and re-layouts  34 us (5%)
  blocking collectives  31 us (5%)
  starting transfers between devices  28.8 us (4%)
  matrix products  17.3 us (3%)
    all_to_all x1, waiting for transfers between devices, exchange_gather(): blocks = lax.all_to_all(blocks, axis, split_axis=0, concat_axis=0)  424 us
    another operation x8, other arithmetic, one_block(): jnp.stack([jnp.cos(angle) * norm_factor, -jnp.sin(angle) * norm_factor],...  72.7 us
    all_to_all x1, blocking collectives, shards(): lax.all_to_all(spectra, 'chan', split_axis=0, concat_axis=3, tiled=True)  31 us
    all_to_all x1, starting transfers between devices, exchange_gather(): blocks = lax.all_to_all(blocks, axis, split_axis=0, concat_axis=0)  19.1 us
    convert_element_type x1, other arithmetic, filter_taps(): return total.astype(jnp.bfloat16)  18.1 us
  transfers between devices with their start and end apart: 3, of which 1 were waited for; matrix products, arithmetic and copies ran while one was open for 15% of the time, Pallas kernels for 0%

profile of v1, /device:TPU:103, one launch (start us, length us, event | category | flops | bytes accessed | tf_op | source)
XLA Modules:
  0.0 659.0 jit_solution(10353528121187602507)
XLA Ops:
  0.0 1.7 convert_element_type.91
  1.7 4.8 collective-permute-start.1
  6.5 0.9 slice.85
  7.4 4.9 collective-permute-start
  12.3 0.0 copy-start.1
  12.3 94.6 %while.13 = (s32[]{:T(128)}, bf16[8,512,2,1024]{3,1,0,2:T(8,128)(2,1)}, s32[8]{0:T(128)S(1)}, s32[]{:T(128)}) while((s32[]{:T(128)}, bf16[8,512,2,1024]{3,1,0,2:T(8,128)(2,1)}, s32[8]{0:T(128)S(1)}, s32[]{:T(128)}) %tuple.40), condition=%wide.region_1.2_spmd.clone, body=%wide.region_0.1_spmd.clone.sunk | while | flops 14156290 | bytes 6295633 | solution.py:46
  12.3 0.6 dynamic_slice.9
  12.9 0.6 iota_add_fusion.2
  13.6 9.1 %fusion.48 = (bf16[1,512,1,1024]{3,1,2,0:T(8,128)(2,1)S(1)}, bf16[1,512,1,1024]{3,1,2,0:T(8,128)(2,1)S(1)}) fusion(s32[512]{0:T(512)S(1)} %iota_add_fusion.2), kind=kLoop, calls=%fused_computation.15.clone.1 | loop fusion | flops 9961472 | bytes 2099200 | tf_op jit(solution)/shard_map/while/body/eval_jaxpr/stack | solution.py:41
  22.7 1.5 fusion.49
  24.2 0.6 dynamic_slice.9
  24.8 0.6 iota_add_fusion.2
  25.4 9.1 %fusion.48 = (bf16[1,512,1,1024]{3,1,2,0:T(8,128)(2,1)S(1)}, bf16[1,512,1,1024]{3,1,2,0:T(8,128)(2,1)S(1)}) fusion(s32[512]{0:T(512)S(1)} %iota_add_fusion.2), kind=kLoop, calls=%fused_computation.15.clone.1 | loop fusion | flops 9961472 | bytes 2099200 | tf_op jit(solution)/shard_map/while/body/eval_jaxpr/stack | solution.py:41
  34.5 1.5 fusion.49
  36.0 0.6 dynamic_slice.9
  36.6 0.6 iota_add_fusion.2
  37.2 9.1 %fusion.48 = (bf16[1,512,1,1024]{3,1,2,0:T(8,128)(2,1)S(1)}, bf16[1,512,1,1024]{3,1,2,0:T(8,128)(2,1)S(1)}) fusion(s32[512]{0:T(512)S(1)} %iota_add_fusion.2), kind=kLoop, calls=%fused_computation.15.clone.1 | loop fusion | flops 9961472 | bytes 2099200 | tf_op jit(solution)/shard_map/while/body/eval_jaxpr/stack | solution.py:41
  46.3 1.5 fusion.49
  47.8 0.6 dynamic_slice.9
  48.4 0.6 iota_add_fusion.2
  49.1 9.1 %fusion.48 = (bf16[1,512,1,1024]{3,1,2,0:T(8,128)(2,1)S(1)}, bf16[1,512,1,1024]{3,1,2,0:T(8,128)(2,1)S(1)}) fusion(s32[512]{0:T(512)S(1)} %iota_add_fusion.2), kind=kLoop, calls=%fused_computation.15.clone.1 | loop fusion | flops 9961472 | bytes 2099200 | tf_op jit(solution)/shard_map/while/body/eval_jaxpr/stack | solution.py:41
  58.2 1.5 fusion.49
  59.6 0.6 dynamic_slice.9
  60.2 0.6 iota_add_fusion.2
  60.9 9.1 %fusion.48 = (bf16[1,512,1,1024]{3,1,2,0:T(8,128)(2,1)S(1)}, bf16[1,512,1,1024]{3,1,2,0:T(8,128)(2,1)S(1)}) fusion(s32[512]{0:T(512)S(1)} %iota_add_fusion.2), kind=kLoop, calls=%fused_computation.15.clone.1 | loop fusion | flops 9961472 | bytes 2099200 | tf_op jit(solution)/shard_map/while/body/eval_jaxpr/stack | solution.py:41
  70.0 1.5 fusion.49
  71.5 0.6 dynamic_slice.9
  72.1 0.6 iota_add_fusion.2
  72.7 9.1 %fusion.48 = (bf16[1,512,1,1024]{3,1,2,0:T(8,128)(2,1)S(1)}, bf16[1,512,1,1024]{3,1,2,0:T(8,128)(2,1)S(1)}) fusion(s32[512]{0:T(512)S(1)} %iota_add_fusion.2), kind=kLoop, calls=%fused_computation.15.clone.1 | loop fusion | flops 9961472 | bytes 2099200 | tf_op jit(solution)/shard_map/while/body/eval_jaxpr/stack | solution.py:41
  81.8 1.5 fusion.49
  83.3 0.6 dynamic_slice.9
  83.9 0.6 iota_add_fusion.2
  84.5 9.1 %fusion.48 = (bf16[1,512,1,1024]{3,1,2,0:T(8,128)(2,1)S(1)}, bf16[1,512,1,1024]{3,1,2,0:T(8,128)(2,1)S(1)}) fusion(s32[512]{0:T(512)S(1)} %iota_add_fusion.2), kind=kLoop, calls=%fused_computation.15.clone.1 | loop fusion | flops 9961472 | bytes 2099200 | tf_op jit(solution)/shard_map/while/body/eval_jaxpr/stack | solution.py:41
  93.6 1.5 fusion.49
  95.1 0.6 dynamic_slice.9
  95.7 0.6 iota_add_fusion.2
  96.3 9.1 %fusion.48 = (bf16[1,512,1,1024]{3,1,2,0:T(8,128)(2,1)S(1)}, bf16[1,512,1,1024]{3,1,2,0:T(8,128)(2,1)S(1)}) fusion(s32[512]{0:T(512)S(1)} %iota_add_fusion.2), kind=kLoop, calls=%fused_computation.15.clone.1 | loop fusion | flops 9961472 | bytes 2099200 | tf_op jit(solution)/shard_map/while/body/eval_jaxpr/stack | solution.py:41
  105.4 1.5 fusion.49
  106.9 0.0 copy-done.1
  106.9 0.6 fusion.30
  107.5 0.0 collective-permute-done
  107.6 0.0 collective-permute-done.1
  107.6 2.9 maximum_convert_fusion
  110.5 6.8 %reshape.232 = f32[32,11,4096]{2,1,0:T(8,128)} reshape(f32[32,45056]{1,0:T(8,128)} %maximum_convert_fusion) | data formatting | bytes 11534336 | tf_op jit(solution)/shard_map/convert_element_type | solution.py:68
  117.3 8.3 %multiply_multiply_fusion = f32[32,11,4096]{2,1,0:T(8,128)} fusion(f32[32,11,4096]{2,1,0:T(8,128)} %reshape.232, f32[32]{0:T(128)S(1)} %convert_element_type.94), kind=kLoop, calls=%fused_computation.18 | loop fusion | flops 2883584 | bytes 11534464 | tf_op jit(solution)/shard_map/mul | solution.py:69
  125.6 18.1 %fusion.13 = bf16[32,4,4096]{2,1,0:T(4,128)(2,1)S(1)} fusion(f32[32,11,4096]{2,1,0:T(8,128)} %multiply_multiply_fusion, f32[4096]{0:T(1024)S(1)} %get-tuple-element.79, f32[4096]{0:T(1024)S(1)} %get-tuple-element.80, f32[4096]{0:T(1024)S(1)} %get-tuple-element.81, f32[4096]{0:T(1024)S(1)} %get-tuple-element.82, f32[4096]{0:T(1024)S(1)} %get-tuple-element.83, ...), kind=kLoop, calls=%fused_computation.24 | loop fusion | flops 8388608 | bytes 17956864 | tf_op jit(solution)/shard_map/convert_element_type | solution.py:53
  143.8 8.7 %fusion.20 = bf16[1024,32,2,4]{0,1,3,2:T(8,128)(2,1)S(1)} fusion(bf16[4096,2,1024,1]{2,0,3,1:T(8,128)(2,1)} %bitcast.46, bf16[32,4,4096]{2,1,0:T(4,128)(2,1)S(1)} %fusion.13), kind=kOutput, calls=%fused_computation.41 | convolution fusion | flops 2147745792 | bytes 18350080 | tf_op jit(solution)/shard_map/isn,nrc->cirs/dot_general | solution.py:72
  152.5 1.4 copy.22
  153.9 2.0 reshape.235
  155.9 31.0 %all_to_all.20 = bf16[32,2,4096]{2,1,0:T(2,128)(2,1)S(1)} all-to-all(bf16[32,2,4096]{2,1,0:T(2,128)(2,1)S(1)} %reshape.235), channel_id=1, replica_groups=mesh['chan'=32,'inp'=16] {'chan'}, dimensions={0} | all-to-all | bytes 1048576 | tf_op jit(solution)/shard_map/all_to_all | solution.py:75
  186.8 1.0 reshape.236
  187.9 1.9 copy.23
  189.8 2.8 copy.26
  192.5 4.3 stack.21
  196.9 19.1 %all-to-all-start.1 = ((bf16[16,32,32,256]{3,2,1,0:T(8,128)(2,1)}), bf16[16,32,32,256]{3,2,1,0:T(8,128)(2,1)}, u32[]{:S(2)}, u32[]{:S(2)}) async-start(bf16[16,32,32,256]{3,2,1,0:T(8,128)(2,1)} %stack.21), calls=%async_computation.1 | async-start | bytes 16777216 | tf_op jit(solution)/shard_map/all_to_all | solution.py:15
  216.0 0.1 fusion.40
  216.1 424.3 %all-to-all-done.1 = bf16[16,32,32,256]{3,2,1,0:T(8,128)(2,1)} async-done(((bf16[16,32,32,256]{3,2,1,0:T(8,128)(2,1)}), bf16[16,32,32,256]{3,2,1,0:T(8,128)(2,1)}, u32[]{:S(2)}, u32[]{:S(2)}) %all-to-all-start.1) | async-done | bytes 8388640 | tf_op jit(solution)/shard_map/all_to_all | solution.py:15
  640.3 8.1 %copy.25 = bf16[32,16,32,256]{3,2,1,0:T(8,128)(2,1)} copy(bf16[32,16,32,256]{3,2,0,1:T(8,128)(2,1)} %bitcast.9) | data formatting | bytes 16777216 | tf_op jit(solution)/shard_map/reshape | solution.py:16
  648.4 0.0 copy-start
  648.4 6.1 convolution_bitcast_fusion.1
  654.5 0.0 copy-done
  654.5 2.5 convolution_bitcast_fusion
  657.0 2.0 fusion.11
  (4 shorter events, 0.0 us)
Async XLA Ops:
  1.7 105.9 %collective-permute-start.1 = (bf16[32,16384]{1,0:T(8,128)(2,1)S(1)}, bf16[32,16384]{1,0:T(8,128)(2,1)S(1)}, u32[]{:S(2)}, u32[]{:S(2)}) collective-permute-start(bf16[32,16384]{1,0:T(8,128)(2,1)S(1)} %convert_element_type.91), channel_id=1, source_target_pairs={{0,16},{16,32},{32,48},{48,64},{64,80},{80,96},{96,112},{112,128},... | collective-permute-start | bytes 3145736 | tf_op jit(solution)/shard_map/ppermute | solution.py:22
  7.4 100.2 %collective-permute-start = (bf16[32,12288]{1,0:T(8,128)(2,1)}, bf16[32,12288]{1,0:T(8,128)(2,1)S(1)}, u32[]{:S(2)}, u32[]{:S(2)}) collective-permute-start(bf16[32,12288]{1,0:T(8,128)(2,1)} %slice.85), channel_id=1, source_target_pairs={{0,32},{16,48},{32,64},{48,80},{64,96},{80,112},{96,128},{112,144}... | collective-permute-start | bytes 2359304 | tf_op jit(solution)/shard_map/ppermute | solution.py:22
  12.3 94.6 %copy-start.1 = (s32[32]{0:T(128)S(1)}, s32[32]{0:T(128)}, u32[]{:S(2)}) copy-start(s32[32]{0:T(128)} %param.5) | copy-start | bytes 388
  196.9 443.5 %all-to-all-start.1 = ((bf16[16,32,32,256]{3,2,1,0:T(8,128)(2,1)}), bf16[16,32,32,256]{3,2,1,0:T(8,128)(2,1)}, u32[]{:S(2)}, u32[]{:S(2)}) async-start(bf16[16,32,32,256]{3,2,1,0:T(8,128)(2,1)} %stack.21), calls=%async_computation.1 | async-start | bytes 16777216 | tf_op jit(solution)/shard_map/all_to_all | solution.py:15
  648.4 6.1 copy-start
